TPU v7x, 256 devices: a whole 4x4x8 slice. The times are simulated.
256 devices in a mesh: dp: 64 (over y, z, core), seq: 4 (over x).
Axes of the slice: x: 4, y: 4, z: 8, core: 2. Of those that a mesh axis runs over, the one named last changes fastest.
Arguments:
- frames: bfloat16 [32768, 1536], P('dp', 'seq')
- owner_slot: int32 [32768], P('dp'), may hold values from -1 to 32767, as said below
- segment: int32 [64, 512], P('dp'), may hold values from 0 to 2, never falling along the last dimension, each value on 1 to 256 neighbouring positions
- norm_gain: float32 [1536], replicated, may hold values from 0.25 to 1.75
- expand: bfloat16 [1536, 2, 1536], P('dp', None, 'seq'), may hold values from -0.15625 to 0.15625
- kernel: float32 [9, 1536], P(None, 'seq'), may hold values from -2.5 to 2.5
- project: bfloat16 [1536, 1536], P('seq', 'dp'), may hold values from -0.15625 to 0.15625
- cotangent: bfloat16 [32768, 1536], P('dp', 'seq'), may hold values from -6 to 6
Outputs:
- output: bfloat16 [32768, 1536], P('dp', 'seq')
- grad_frames: bfloat16 [32768, 1536], P('dp', 'seq')
- grad_gain: float32 [1536], P('seq')
- grad_kernel: float32 [9, 1536], P(None, 'seq')
- grad_expand: float32 [1536, 2, 1536], P('dp', None, 'seq')
- grad_project: float32 [1536, 1536], P('seq', 'dp')
Inputs may be any that keep to these rules, and one draw needn't show every extreme that they name: `owner_slot`: for each arrival row, the balanced row that takes it, or -1 for an empty arrival row; no balanced row is named twice. The live rows of each pack come first, contiguous, ordered by sending index of dp and then by arrival row; empty rows fill the pack's tail. Of the 512 arrival rows of one index of dp, at most 8 name rows of any one pack; some pack takes exactly 8 rows from every index of dp. `segment`: within each pack the utterance numbers never fall; a pack holds 3 utterances of 1 to 256 frames, one of exactly 256.
All inputs are finite; a program needn't handle non-finite values.
Results may differ from a plain program's by a relative error of at most 0.01.
Values may be sent and summed in bfloat16 or wider, within the bound.
No kernel may reach another device: no remote copies, remote signals or barrier semaphores. Data moves between devices by JAX's collectives and lax.ppermute only.
A program may use at most 128 MiB of HBM per device.

v0:
```python
import math
import jax
import jax.numpy as jnp
from jax import lax
from jax.sharding import PartitionSpec as P

D = 1536
KSIZE = 9
EPS = 1e-05


def conv_masks(labels):
    half_width = (KSIZE - 1) // 2
    length = labels.shape[0]
    padded = jnp.pad(labels, (half_width, half_width), constant_values=-1)
    return [
        (padded[tap_index : tap_index + length] == labels).astype(jnp.float32)[:, None]
        for tap_index in range(KSIZE)
    ]


def depthwise(signal, kernel, tap_masks):
    half_width = (KSIZE - 1) // 2
    length = signal.shape[0]
    padded = jnp.pad(signal, ((half_width, half_width), (0, 0)))
    total = jnp.zeros(signal.shape, jnp.float32)
    for tap_index in range(KSIZE):
        total = (
            total
            + kernel[tap_index] * padded[tap_index : tap_index + length] * tap_masks[tap_index]
        )
    return total


def depthwise_back(signal, upstream, kernel, tap_masks):
    half_width = (KSIZE - 1) // 2
    length = signal.shape[0]
    padded = jnp.pad(signal, ((half_width, half_width), (0, 0)))
    spread = jnp.zeros((length + 2 * half_width, signal.shape[1]), jnp.float32)
    tap_sums = []
    for tap_index in range(KSIZE):
        masked = upstream * tap_masks[tap_index]
        tap_sums.append(jnp.sum(masked * padded[tap_index : tap_index + length], axis=0))
        spread = spread + jnp.pad(
            kernel[tap_index] * masked, ((tap_index, 2 * half_width - tap_index), (0, 0))
        )
    return (jnp.stack(tap_sums), spread[half_width : half_width + length])


def place_rows(incoming, landing, row_count):
    flat = incoming.reshape(-1, incoming.shape[-1])
    total_slots = flat.shape[0]
    inverse = (
        jnp.full((row_count + 1,), total_slots, jnp.int32)
        .at[landing.reshape(-1)]
        .set(jnp.arange(total_slots, dtype=jnp.int32))[:row_count]
    )
    padded = jnp.concatenate([flat, jnp.zeros((1, flat.shape[1]), flat.dtype)])
    return (padded[inverse], inverse < total_slots)


def shards(frames, owner_slot, segment, norm_gain, expand, kernel, project, cotangent):
    row_count, quarter = frames.shape
    groups = lax.axis_size("dp")
    lane_index = lax.axis_index("seq")
    capacity = row_count // groups
    bucket_slots = groups * capacity
    dest_group = jnp.where(owner_slot >= 0, owner_slot // row_count, groups)
    onehot = (dest_group[:, None] == jnp.arange(groups, dtype=jnp.int32)[None, :]).astype(jnp.int32)
    earlier = jnp.cumsum(onehot, axis=0) - onehot
    within = jnp.sum(earlier * onehot, axis=1)
    send_pos = jnp.where(owner_slot >= 0, dest_group * capacity + within, bucket_slots)
    source_row = (
        jnp.full((bucket_slots + 1,), row_count, jnp.int32)
        .at[send_pos]
        .set(jnp.arange(row_count, dtype=jnp.int32))[:bucket_slots]
    )
    slot_padded = jnp.concatenate([owner_slot, jnp.full((1,), -1, jnp.int32)])
    named_slot = slot_padded[source_row]
    landing_out = jnp.where(named_slot >= 0, named_slot % row_count, row_count).reshape(
        groups, capacity
    )
    padded_in = jnp.concatenate([frames, jnp.zeros((1, quarter), jnp.bfloat16)])
    outgoing = padded_in[source_row].reshape(groups, capacity, quarter)
    incoming, landing = (
        lax.all_to_all(outgoing, "dp", split_axis=0, concat_axis=0, tiled=True),
        lax.all_to_all(landing_out, "dp", split_axis=0, concat_axis=0, tiled=True),
    )
    local_rows, occupied = place_rows(incoming, landing, row_count)
    whole_rows = lax.all_gather(local_rows, "seq", axis=1, tiled=True)
    live_col = occupied.astype(jnp.float32)[:, None]
    floats = whole_rows.astype(jnp.float32)
    row_mean = jnp.mean(floats, axis=1, keepdims=True)
    centred = floats - row_mean
    inv_scale = lax.rsqrt(jnp.mean(centred * centred, axis=1, keepdims=True) + EPS)
    normed = centred * inv_scale
    scaled = (normed * norm_gain).astype(jnp.bfloat16)
    expand_full = lax.all_gather(expand, "dp", axis=0, tiled=True).reshape(D, 2 * quarter)
    project_full = lax.all_gather(project, "dp", axis=1, tiled=True)
    joined = jnp.dot(scaled, expand_full, preferred_element_type=jnp.float32)
    value_half = joined[:, :quarter]
    gate_sig = jax.nn.sigmoid(joined[:, quarter:])
    glu_out = value_half * gate_sig
    tap_masks = conv_masks(segment[0])
    conv_out = depthwise(glu_out, kernel, tap_masks)
    conv_sig = jax.nn.sigmoid(conv_out)
    hidden = (conv_out * conv_sig * live_col).astype(jnp.bfloat16)
    partial_out = jnp.dot(hidden, project_full, preferred_element_type=jnp.float32)
    mixed_share = lax.psum_scatter(
        partial_out.astype(jnp.bfloat16), "seq", scatter_dimension=1, tiled=True
    ).astype(jnp.float32)
    output = (local_rows.astype(jnp.float32) + mixed_share).astype(jnp.bfloat16)
    inv_root = 1.0 / math.sqrt(row_count * groups)
    cot_full = lax.all_gather(cotangent, "seq", axis=1, tiled=True)
    project_term = lax.dot_general(
        hidden, cot_full, (((0,), (0,)), ((), ())), preferred_element_type=jnp.float32
    )
    grad_project = lax.psum_scatter(project_term, "dp", scatter_dimension=1, tiled=True) * inv_root
    hidden_grad = (
        lax.dot_general(
            cot_full, project_full, (((1,), (1,)), ((), ())), preferred_element_type=jnp.float32
        )
        * live_col
    )
    conv_grad = hidden_grad * (conv_sig + conv_out * conv_sig * (1.0 - conv_sig))
    kernel_term, glu_grad = depthwise_back(glu_out, conv_grad, kernel, tap_masks)
    proj_grad = jnp.concatenate(
        [glu_grad * gate_sig, glu_grad * value_half * gate_sig * (1.0 - gate_sig)], axis=1
    ).astype(jnp.bfloat16)
    term_block = lax.dot_general(
        scaled, proj_grad, (((0,), (0,)), ((), ())), preferred_element_type=jnp.float32
    )
    grad_expand = (
        lax.psum_scatter(
            term_block.reshape(expand.shape[0] * lax.axis_size("dp"), 2, quarter),
            "dp",
            scatter_dimension=0,
            tiled=True,
        )
        * inv_root
    )
    scaled_part = lax.dot_general(
        proj_grad, expand_full, (((1,), (1,)), ((), ())), preferred_element_type=jnp.float32
    )
    normed_local = lax.dynamic_slice_in_dim(normed, lane_index * quarter, quarter, 1)
    scaled_grad = lax.psum(scaled_part.astype(jnp.bfloat16), "seq").astype(jnp.float32)
    normed_grad = scaled_grad * norm_gain
    first_mean = jnp.mean(normed_grad, axis=1, keepdims=True)
    second_mean = jnp.mean(normed_grad * normed, axis=1, keepdims=True)
    full_grad = inv_scale * (normed_grad - first_mean - normed * second_mean)
    packed_grad = lax.dynamic_slice_in_dim(full_grad, lane_index * quarter, quarter, 1)
    scaled_share = lax.dynamic_slice_in_dim(scaled_grad, lane_index * quarter, quarter, 1)
    gain_term = jnp.sum(scaled_share * normed_local, axis=0)
    gain_sum, kernel_sum = lax.psum((gain_term, kernel_term), "dp")
    back_rows = (packed_grad + cotangent.astype(jnp.float32)).astype(jnp.bfloat16)
    back_padded = jnp.concatenate([back_rows, jnp.zeros((1, quarter), jnp.bfloat16)])
    returning = back_padded[landing.reshape(-1)].reshape(groups, capacity, quarter)
    returned = lax.all_to_all(returning, "dp", split_axis=0, concat_axis=0, tiled=True)
    returned_flat = jnp.concatenate(
        [returned.reshape(bucket_slots, quarter), jnp.zeros((1, quarter), jnp.bfloat16)]
    )
    grad_frames = returned_flat[send_pos]
    return (
        output,
        grad_frames,
        gain_sum * inv_root,
        kernel_sum * inv_root,
        grad_expand,
        grad_project,
    )


def solution(mesh):
    placed = (
        P("dp", "seq"),
        P("dp"),
        P("dp", None),
        P(),
        P("dp", None, "seq"),
        P(None, "seq"),
        P("seq", "dp"),
        P("dp", "seq"),
    )
    return jax.shard_map(
        shards,
        mesh=mesh,
        in_specs=placed,
        out_specs=(
            P("dp", "seq"),
            P("dp", "seq"),
            P("seq"),
            P(None, "seq"),
            P("dp", None, "seq"),
            P("seq", "dp"),
        ),
        check_vma=False,
    )
```

profile of v0, /device:TPU:4, one launch (start us, length us, event | category | flops | bytes accessed | tf_op | source)
XLA Modules:
  0.0 722.8 jit_solution(6718990988851698500)
XLA Ops:
  7.2 0.7 fusion.22
  7.9 0.7 fusion.55
  8.6 1.2 reduce-window.6
  9.8 0.2 slice_reduce_fusion
  10.2 0.7 compare_select_fusion.3
  10.9 2.4 scatter_custom_fusion
  13.4 0.7 pad_add_fusion.7
  14.1 2.3 gather_fusion.1
  16.5 0.6 fusion.20
  17.1 12.1 %all-to-all-start.1 = ((s32[64,1,8]{2,1,0:T(1,128)}), s32[64,1,8]{2,1,0:T(1,128)S(1)}, u32[]{:S(2)}, u32[]{:S(2)}) async-start(s32[64,1,8]{2,1,0:T(1,128)} %bitcast.4), calls=%async_computation.1 | async-start | bytes 65536 | tf_op jit(solution)/shard_map/all_to_all | solution.py:87
  29.3 2.6 gather_fusion
  31.9 6.8 all-to-all-done.1
  38.7 4.6 all-to-all-start
  43.4 0.5 broadcast.267
  43.9 0.7 reduce.23
  44.8 2.4 scatter_custom_fusion.1
  47.2 10.6 %all-to-all-done = bf16[64,8,384]{2,1,0:T(8,128)(2,1)S(1)} async-done(((bf16[64,8,384]{2,1,0:T(8,128)(2,1)}), bf16[64,8,384]{2,1,0:T(8,128)(2,1)S(1)}, u32[]{:S(2)}, u32[]{:S(2)}) %all-to-all-start) | async-done | bytes 393248 | tf_op jit(solution)/shard_map/all_to_all | solution.py:86
  57.9 2.6 gather_fusion.2
  60.6 0.7 all-gather.6.cloned.1.call-update
  61.3 0.7 all-gather.8.cloned.1.call-update
  62.0 0.5 all-gather.10.cloned.1.call-update
  62.6 0.2 all-reduce.21.cloned.1.call-start
  63.0 22.6 %all-gather.12.cloned.1.call-done = bf16[512,1536]{1,0:T(8,128)(2,1)} async-done(((bf16[512,384]{1,0:T(8,128)(2,1)}), bf16[512,1536]{1,0:T(8,128)(2,1)}) %all-gather.12.cloned.1.call-update) | async-done | bytes 1572880 | tf_op jit(solution)/shard_map/all_gather | solution.py:90
  85.6 1.8 convert_reduce_fusion
  87.4 0.5 fusion.2
  88.0 79.3 %all-gather.6.cloned.1.call-done = bf16[1536,2,384]{2,1,0:T(2,128)(2,1)} async-done(((bf16[24,2,384]{2,1,0:T(2,128)(2,1)}), bf16[1536,2,384]{2,1,0:T(2,128)(2,1)}) %all-gather.6.cloned.1.call-update) | async-done | bytes 2359312 | tf_op jit(solution)/shard_map/all_gather | solution.py:98
  167.3 2.1 copy.23
  169.5 1.5 fusion.13
  171.0 0.2 slice_multiply_fusion
  171.2 0.9 copy-done.3
  172.1 2.0 multiply_add_fusion
  174.1 70.2 %all-gather.8.cloned.1.call-done = bf16[384,1536]{0,1:T(8,128)(2,1)} async-done(((bf16[384,24]{0,1:T(8,128)(2,1)}), bf16[384,1536]{0,1:T(8,128)(2,1)}) %all-gather.8.cloned.1.call-update) | async-done | bytes 1179664 | tf_op jit(solution)/shard_map/all_gather | solution.py:99
  244.4 27.2 %all-gather.10.cloned.1.call-done = bf16[512,1536]{1,0:T(8,128)(2,1)} async-done(((bf16[512,384]{1,0:T(8,128)(2,1)}), bf16[512,1536]{1,0:T(8,128)(2,1)}) %all-gather.10.cloned.1.call-update) | async-done | bytes 1572880 | tf_op jit(solution)/shard_map/all_gather | solution.py:114
  271.6 7.9 %multiply_reduce_fusion.1 = (f32[384]{0:T(512)}, f32[384]{0:T(512)}, f32[384]{0:T(512)}, f32[384]{0:T(512)}, f32[384]{0:T(512)}, /*index=5*/f32[384]{0:T(512)}, ...) fusion(f32[512,384]{1,0:T(8,128)} %copy-done.3, ...), kind=kOutput, calls=%fused_computation.36 | convolution fusion | flops 611054208 | bytes 5932032 | tf_op jit(solution)/shard_map/dot_general | solution.py:120
  279.5 0.7 multiply_multiply_fusion.7
  280.4 0.6 multiply_convert_fusion.2
  281.0 0.2 multiply_convert_fusion.1
  281.3 0.7 copy-done.8
  282.0 0.8 copy-done.5
  282.8 2.6 convolution_convert_fusion
  285.5 4.8 fusion.12
  290.3 8.2 %copy.19 = f32[1536,2,384]{2,1,0:T(2,128)} copy(f32[1536,2,384]{0,2,1:T(8,128)} %bitcast.41) | data formatting | bytes 9437184 | tf_op jit(solution)/shard_map/reshape | solution.py:135
  298.5 0.6 copy-done.26
  299.1 2.6 convolution_convert_fusion.1
  301.7 1.6 copy.20
  303.3 0.3 reduce-scatter.9.cloned.1.call-start
  303.5 4.2 fusion.46
  307.7 0.6 copy-done.13
  308.4 32.9 %all-reduce.21.cloned.1.call-done = bf16[512,1536]{1,0:T(8,128)(2,1)} async-done(((bf16[512,1536]{1,0:T(8,128)(2,1)}), bf16[512,1536]{1,0:T(8,128)(2,1)}) %all-reduce.21.cloned.1.call-update) | async-done | bytes 1572880 | tf_op jit(solution)/shard_map/psum | solution.py:146
  341.3 1.9 convert_element_type.110
  343.2 1.1 fusion.11
  344.3 0.4 multiply_reduce_fusion.10
  344.8 2.6 gather_fusion.3
  347.4 10.5 %all-to-all-start.2 = ((bf16[64,8,384]{2,1,0:T(8,128)(2,1)}), bf16[64,8,384]{2,1,0:T(8,128)(2,1)S(1)}, u32[]{:S(2)}, u32[]{:S(2)}) async-start(bf16[64,8,384]{2,1,0:T(8,128)(2,1)} %bitcast.7), calls=%async_computation.2 | async-start | bytes 786432 | tf_op jit(solution)/shard_map/all_to_all | solution.py:158
  357.9 0.6 dynamic-slice
  359.4 251.8 %all-reduce.17 = (f32[384]{0:T(512)S(1)}, f32[9,384]{1,0:T(8,128)S(1)}) all-reduce(f32[384]{0:T(512)S(1)} %get-tuple-element.30, f32[9,384]{1,0:T(8,128)S(1)} %stack.39), channel_id=1, replica_groups=mesh['dp'=64,'seq'=4] {'dp'}, use_global_device_ids=true, to_apply=%region_12.13 | all-reduce | flops 3840 | bytes 30720 | tf_op jit(solution)/shard_map/psum | solution.py:154
  611.2 0.6 broadcast_multiply_fusion.4
  611.8 0.6 broadcast_multiply_fusion.3
  612.4 2.6 gather_fusion.4
  615.0 1.6 dynamic-slice_multiply_fusion
  616.6 1.2 copy.21
  617.8 0.8 add_convert_fusion
  618.6 95.9 %reduce-scatter.9.cloned.1.call-done = f32[384,24]{0,1:T(8,128)} async-done(((f32[384,1536]{0,1:T(8,128)}), f32[384,24]{0,1:T(8,128)}) %reduce-scatter.9.cloned.1.call-update) | async-done | bytes 36880
  714.6 1.4 broadcast_multiply_fusion.2
  (101 shorter events, 1.5 us)
Async XLA Ops:
  7.2 22.1 %copy-start.7 = (bf16[512,384]{1,0:T(8,128)(2,1)S(1)}, bf16[512,384]{1,0:T(8,128)(2,1)}, u32[]{:S(2)}) copy-start(bf16[512,384]{1,0:T(8,128)(2,1)} %param.8) | copy-start | bytes 1179652
  10.9 3.2 copy-start.10
  17.1 21.6 %all-to-all-start.1 = ((s32[64,1,8]{2,1,0:T(1,128)}), s32[64,1,8]{2,1,0:T(1,128)S(1)}, u32[]{:S(2)}, u32[]{:S(2)}) async-start(s32[64,1,8]{2,1,0:T(1,128)} %bitcast.4), calls=%async_computation.1 | async-start | bytes 65536 | tf_op jit(solution)/shard_map/all_to_all | solution.py:87
  38.7 19.1 %all-to-all-start = ((bf16[64,8,384]{2,1,0:T(8,128)(2,1)}), bf16[64,8,384]{2,1,0:T(8,128)(2,1)S(1)}, u32[]{:S(2)}, u32[]{:S(2)}) async-start(bf16[64,8,384]{2,1,0:T(8,128)(2,1)} %bitcast.2), calls=%async_computation | async-start | bytes 786432 | tf_op jit(solution)/shard_map/all_to_all | solution.py:86
  43.3 42.2 %all-gather.12.cloned.1.call-start = ((), (), s32[]{:S(2)}) async-start(), calls=%async_computation.9 | async-start | bytes 1966080 | tf_op jit(solution)/shard_map/all_gather | solution.py:90
  44.7 13.1 %copy-start.12 = (s32[512,1]{0,1:T(1,128)}, s32[512,1]{0,1:T(1,128)S(1)}, u32[]{:S(2)}) copy-start(s32[512,1]{0,1:T(1,128)S(1)} %compare_select_fusion) | copy-start | bytes 6148
  57.9 4.9 copy-start.14
  57.9 5.0 copy-start.15
  60.5 106.8 %all-gather.6.cloned.1.call-start = ((), (), s32[]{:S(2)}) async-start(), calls=%async_computation.5 | async-start | bytes 2396160 | tf_op jit(solution)/shard_map/all_gather | solution.py:98
  61.3 183.1 %all-gather.8.cloned.1.call-start = ((), (), s32[]{:S(2)}) async-start(), calls=%async_computation.6 | async-start | bytes 1198080 | tf_op jit(solution)/shard_map/all_gather | solution.py:99
  62.0 209.6 %all-gather.10.cloned.1.call-start = ((), (), s32[]{:S(2)}) async-start(), calls=%async_computation.7 | async-start | bytes 1966080 | tf_op jit(solution)/shard_map/all_gather | solution.py:114
  62.6 278.7 %all-reduce.21.cloned.1.call-start = ((), (), s32[]{:S(2)}) async-start(), calls=%async_computation.8 | async-start | bytes 3145728 | tf_op jit(solution)/shard_map/psum | solution.py:146
  63.0 208.7 %copy-start.25 = (f32[512]{0:T(512)}, f32[512]{0:T(512)S(1)}, u32[]{:S(2)}) copy-start(f32[512]{0:T(512)S(1)} %compare_convert_fusion) | copy-start | bytes 6148
  85.6 1.9 copy-start
  167.3 2.2 copy-start.9
  169.5 1.5 copy-start.4
  171.2 0.9 copy-start.3
  281.0 1.8 copy-start.5
  281.3 0.7 copy-start.8
  285.5 329.6 %all-reduce.23.cloned.1.call-start = ((), (), s32[]{:S(2)}) async-start(), calls=%async_computation.11 | async-start | bytes 9437184
  298.4 0.7 copy-start.26
  298.4 318.1 %reduce-scatter.7.cloned.1.call-start = ((), (), s32[]{:S(2)}) async-start(), calls=%async_computation.10 | async-start | bytes 1966080
  303.3 411.3 %reduce-scatter.9.cloned.1.call-start = ((), (), s32[]{:S(2)}) async-start(), calls=%async_computation.12 | async-start | bytes 2396160
  307.7 0.7 copy-start.13
  341.3 1.9 copy-start.1
  343.2 1.1 copy-start.6
  344.7 13.2 %copy-start.27 = (u32[256]{0:T(256)S(1)}, u32[256]{0:T(256)}, u32[]{:S(2)}) copy-start(u32[256]{0:T(256)} %constant.110) | copy-start | bytes 3076
  344.7 14.4 %copy-start.11 = (s32[512]{0:T(512)S(1)}, s32[512]{0:T(512)}, u32[]{:S(2)}) copy-start(s32[512]{0:T(512)} %copy-done.10) | copy-start | bytes 6148
  344.7 14.4 %copy-start.24 = (f32[384]{0:T(512)S(1)}, f32[384]{0:T(512)}, u32[]{:S(2)}) copy-start(f32[384]{0:T(512)} %get-tuple-element.9) | copy-start | bytes 4612
  344.8 14.4 %copy-start.23 = (f32[384]{0:T(512)S(1)}, f32[384]{0:T(512)}, u32[]{:S(2)}) copy-start(f32[384]{0:T(512)} %get-tuple-element.10) | copy-start | bytes 4612
  344.8 14.4 %copy-start.22 = (f32[384]{0:T(512)S(1)}, f32[384]{0:T(512)}, u32[]{:S(2)}) copy-start(f32[384]{0:T(512)} %get-tuple-element.11) | copy-start | bytes 4612
  344.8 14.5 %copy-start.21 = (f32[384]{0:T(512)S(1)}, f32[384]{0:T(512)}, u32[]{:S(2)}) copy-start(f32[384]{0:T(512)} %get-tuple-element.12) | copy-start | bytes 4612
  344.8 14.5 %copy-start.20 = (f32[384]{0:T(512)S(1)}, f32[384]{0:T(512)}, u32[]{:S(2)}) copy-start(f32[384]{0:T(512)} %get-tuple-element.16) | copy-start | bytes 4612
  344.8 14.5 %copy-start.19 = (f32[384]{0:T(512)S(1)}, f32[384]{0:T(512)}, u32[]{:S(2)}) copy-start(f32[384]{0:T(512)} %get-tuple-element.13) | copy-start | bytes 4612
  344.8 14.5 %copy-start.18 = (f32[384]{0:T(512)S(1)}, f32[384]{0:T(512)}, u32[]{:S(2)}) copy-start(f32[384]{0:T(512)} %get-tuple-element.14) | copy-start | bytes 4612
  344.8 14.5 %copy-start.17 = (f32[384]{0:T(512)S(1)}, f32[384]{0:T(512)}, u32[]{:S(2)}) copy-start(f32[384]{0:T(512)} %get-tuple-element.15) | copy-start | bytes 4612
  344.8 14.5 %copy-start.16 = (f32[384]{0:T(512)S(1)}, f32[384]{0:T(512)}, u32[]{:S(2)}) copy-start(f32[384]{0:T(512)} %get-tuple-element.8) | copy-start | bytes 4612
  347.4 265.0 %all-to-all-start.2 = ((bf16[64,8,384]{2,1,0:T(8,128)(2,1)}), bf16[64,8,384]{2,1,0:T(8,128)(2,1)S(1)}, u32[]{:S(2)}, u32[]{:S(2)}) async-start(bf16[64,8,384]{2,1,0:T(8,128)(2,1)} %bitcast.7), calls=%async_computation.2 | async-start | bytes 786432 | tf_op jit(solution)/shard_map/all_to_all | solution.py:158
  612.4 5.4 copy-start.2
Sparse Core Ops, SparseCore 0:
  60.6 24.8 all-gather.11
  88.2 79.0 all-gather.5
  170.0 74.3 all-gather.7
  246.1 25.4 all-gather.9
  285.6 55.6 all-reduce.20
  344.7 201.8 all-reduce.22
  549.1 25.4 reduce-scatter.6
  578.7 135.7 reduce-scatter.8
where the time goes:
time: 724 us; the launch traced here: 723 us
  waiting for transfers between devices  348 us (48%)
  blocking collectives  252 us (35%)
  local copies, waits for them, and re-layouts  36.2 us (5%)
  starting transfers between devices  27.9 us (4%)
  matrix products  23.5 us (3%)
  other arithmetic  20.3 us (3%)
  between operations  15.4 us (2%)
    psum x1, blocking collectives, shards(): gain_sum, kernel_sum = lax.psum((gain_term, kernel_term), 'dp')  252 us
    unnamed x11, waiting for transfers between devices  97.9 us
    all_gather x1, waiting for transfers between devices, shards(): lax.all_gather(expand, 'dp', axis=0, tiled=True).reshape(D, 2 * quarter)  79.3 us
    all_gather x1, waiting for transfers between devices, shards(): project_full = lax.all_gather(project, 'dp', axis=1, tiled=True)  70.2 us
    psum x1, waiting for transfers between devices, shards(): lax.psum(scaled_part.astype(jnp.bfloat16), 'seq').astype(jnp.float32)  32.9 us
    all_gather x1, waiting for transfers between devices, shards(): cot_full = lax.all_gather(cotangent, 'seq', axis=1, tiled=True)  27.2 us
    all_gather x1, waiting for transfers between devices, shards(): whole_rows = lax.all_gather(local_rows, 'seq', axis=1, tiled=True)  22.6 us
  transfers between devices with their start and end apart: 11, of which 8 were waited for; matrix products, arithmetic and copies ran while one was open for 7% of the time, Pallas kernels for 0%

commit v1 on v0

--- a/solution.py
+++ b/solution.py
@@ -111,7 +111,28 @@
     ).astype(jnp.float32)
     output = (local_rows.astype(jnp.float32) + mixed_share).astype(jnp.bfloat16)
     inv_root = 1.0 / math.sqrt(row_count * groups)
-    cot_full = lax.all_gather(cotangent, "seq", axis=1, tiled=True)
+
+    def map_runs_on_mesh(t0):
+        main, local_next, big = (lax.axis_size("seq"), lax.axis_index("seq"), t0.shape[1])
+        pieces_in = [(src_i, (src_i + 1) % main) for src_i in range(main)]
+        gallery = [(src_i, (src_i - 1) % main) for src_i in range(main)]
+        next_value = jnp.zeros((*t0.shape[:1], main * big, *t0.shape[2:]), t0.dtype)
+        new = value_now = t0
+        m_next = main // 2
+        next_value = lax.dynamic_update_slice_in_dim(next_value, t0, local_next * big, axis=1)
+        for i0 in range(1, m_next + 1):
+            new = lax.ppermute(new, "seq", pieces_in)
+            next_value = lax.dynamic_update_slice_in_dim(
+                next_value, new, (local_next - i0) % main * big, axis=1
+            )
+            if i0 < main - m_next:
+                value_now = lax.ppermute(value_now, "seq", gallery)
+                next_value = lax.dynamic_update_slice_in_dim(
+                    next_value, value_now, (local_next + i0) % main * big, axis=1
+                )
+        return next_value
+
+    cot_full = map_runs_on_mesh(cotangent)
     project_term = lax.dot_general(
         hidden, cot_full, (((0,), (0,)), ((), ())), preferred_element_type=jnp.float32
     )

time: 724 us -> 699 us (0.965)
  waiting for transfers between devices: 348 us -> 315 us
    all_gather x1 -> x0, waiting for transfers between devices: 27.2 us -> none  [shards(): cot_full = lax.all_gather(cotangent, 'seq', axis=1, tiled=True)]
    ppermute x0 -> x3, waiting for transfers between devices: none -> 27.1 us  [the longest x2 27.1 us: map_runs_on_mesh(): new = lax.ppermute(new, 'seq', pieces_in)]
    all_gather x1, waiting for transfers between devices: 22.6 us -> 0.01 us  [shards(): whole_rows = lax.all_gather(local_rows, 'seq', axis=1, tiled=True)]
    unnamed x11 -> x10, waiting for transfers between devices: 97.9 us -> 96.5 us
  transfers between devices with their start and end apart: 11 -> 13, of which waited for: 8 -> 8; matrix products, arithmetic and copies ran while one was open for 7% -> 7% of each run, Pallas kernels for 0% -> 0%
where the time goes in v1:
time: 699 us; the launch traced here: 698 us
  waiting for transfers between devices  315 us (45%)
  blocking collectives  252 us (36%)
  local copies, waits for them, and re-layouts  40.3 us (6%)
  starting transfers between devices  30.5 us (4%)
  matrix products  22.8 us (3%)
  other arithmetic  22.1 us (3%)
  between operations  15.8 us (2%)
    psum x1, blocking collectives, shards(): gain_sum, kernel_sum = lax.psum((gain_term, kernel_term), 'dp')  252 us
    unnamed x10, waiting for transfers between devices  96.5 us
    all_gather x1, waiting for transfers between devices, shards(): lax.all_gather(expand, 'dp', axis=0, tiled=True).reshape(D, 2 * quarter)  75.8 us
    all_gather x1, waiting for transfers between devices, shards(): project_full = lax.all_gather(project, 'dp', axis=1, tiled=True)  69.2 us
    psum x1, waiting for transfers between devices, shards(): lax.psum(scaled_part.astype(jnp.bfloat16), 'seq').astype(jnp.float32)  29 us
    ppermute x2, waiting for transfers between devices, map_runs_on_mesh(): new = lax.ppermute(new, 'seq', pieces_in)  27.1 us
  transfers between devices with their start and end apart: 13, of which 8 were waited for; matrix products, arithmetic and copies ran while one was open for 7% of the time, Pallas kernels for 0%

profile of v1, /device:TPU:4, one launch (start us, length us, event | category | flops | bytes accessed | tf_op | source)
XLA Modules:
  0.0 698.3 jit_solution(10989659867946944871)
XLA Ops:
  7.2 0.7 fusion.22
  7.9 0.7 fusion.55
  8.6 1.2 reduce-window.6
  10.2 0.7 compare_select_fusion.3
  10.9 2.4 scatter_custom_fusion
  13.4 0.7 pad_add_fusion.7
  14.1 2.3 gather_fusion.1
  16.5 0.6 fusion.20
  17.1 12.1 %all-to-all-start.1 = ((s32[64,1,8]{2,1,0:T(1,128)}), s32[64,1,8]{2,1,0:T(1,128)S(1)}, u32[]{:S(2)}, u32[]{:S(2)}) async-start(s32[64,1,8]{2,1,0:T(1,128)} %bitcast.4), calls=%async_computation.1 | async-start | bytes 65536 | tf_op jit(solution)/shard_map/all_to_all | solution.py:87
  29.3 2.6 gather_fusion
  31.9 6.8 all-to-all-done.1
  38.7 4.6 all-to-all-start
  43.4 0.5 broadcast.274
  43.9 0.7 reduce.23
  44.8 2.4 scatter_custom_fusion.1
  47.2 10.6 %all-to-all-done = bf16[64,8,384]{2,1,0:T(8,128)(2,1)S(1)} async-done(((bf16[64,8,384]{2,1,0:T(8,128)(2,1)}), bf16[64,8,384]{2,1,0:T(8,128)(2,1)S(1)}, u32[]{:S(2)}, u32[]{:S(2)}) %all-to-all-start) | async-done | bytes 393248 | tf_op jit(solution)/shard_map/all_to_all | solution.py:86
  57.9 2.6 gather_fusion.2
  60.5 0.7 all-gather.5.cloned.1.call-update
  61.3 1.3 collective-permute-start
  62.6 0.8 collective-permute-start.1
  63.7 0.7 fusion.43
  64.4 0.6 slice_reduce_fusion.9
  65.0 9.2 %collective-permute-done = bf16[512,384]{1,0:T(8,128)(2,1)S(1)} collective-permute-done((bf16[512,384]{1,0:T(8,128)(2,1)S(1)}, bf16[512,384]{1,0:T(8,128)(2,1)S(1)}, u32[]{:S(2)}, u32[]{:S(2)}) %collective-permute-start) | collective-permute-done | bytes 393248 | tf_op jit(solution)/shard_map/ppermute | solution.py:124
  74.1 0.7 collective-permute-start.2
  74.8 0.6 compare_convert_fusion
  75.5 17.9 %collective-permute-done.2 = bf16[512,384]{1,0:T(8,128)(2,1)S(1)} collective-permute-done((bf16[512,384]{1,0:T(8,128)(2,1)S(1)}, bf16[512,384]{1,0:T(8,128)(2,1)S(1)}, u32[]{:S(2)}, u32[]{:S(2)}) %collective-permute-start.2) | collective-permute-done | bytes 393248 | tf_op jit(solution)/shard_map/ppermute | solution.py:124
  93.6 1.2 copy-done.6
  94.7 1.8 convert_reduce_fusion
  96.6 0.5 fusion.2
  97.1 0.6 add_rsqrt_fusion
  97.7 75.8 %all-gather.5.cloned.1.call-done = bf16[1536,2,384]{2,1,0:T(2,128)(2,1)} async-done(((bf16[24,2,384]{2,1,0:T(2,128)(2,1)}), bf16[1536,2,384]{2,1,0:T(2,128)(2,1)}) %all-gather.5.cloned.1.call-update) | async-done | bytes 2359312 | tf_op jit(solution)/shard_map/all_gather | solution.py:98
  173.5 2.2 copy.23
  175.7 2.2 fusion.13
  178.3 0.9 copy-done.3
  179.3 2.0 multiply_add_fusion
  181.4 69.2 %all-gather.7.cloned.1.call-done = bf16[384,1536]{0,1:T(8,128)(2,1)} async-done(((bf16[384,24]{0,1:T(8,128)(2,1)}), bf16[384,1536]{0,1:T(8,128)(2,1)}) %all-gather.7.cloned.1.call-update) | async-done | bytes 1179664 | tf_op jit(solution)/shard_map/all_gather | solution.py:99
  250.7 7.9 %multiply_reduce_fusion.1 = (f32[384]{0:T(512)}, f32[384]{0:T(512)}, f32[384]{0:T(512)}, f32[384]{0:T(512)}, f32[384]{0:T(512)}, /*index=5*/f32[384]{0:T(512)}, ...) fusion(f32[512,384]{1,0:T(8,128)} %copy-done.3, ...), kind=kOutput, calls=%fused_computation.36 | convolution fusion | flops 611054208 | bytes 5932032 | tf_op jit(solution)/shard_map/dot_general | solution.py:141
  258.7 0.7 multiply_multiply_fusion.7
  259.6 0.6 multiply_convert_fusion.2
  261.2 0.9 copy-done.5
  262.2 2.6 convolution_convert_fusion
  264.9 0.9 copy-done.10
  265.9 3.8 fusion.12
  269.6 8.2 %copy.19 = f32[1536,2,384]{2,1,0:T(2,128)} copy(f32[1536,2,384]{0,2,1:T(8,128)} %bitcast.41) | data formatting | bytes 9437184 | tf_op jit(solution)/shard_map/reshape | solution.py:156
  277.9 2.6 convolution_convert_fusion.1
  280.6 1.6 copy.20
  282.5 1.1 copy-done.7
  283.6 3.6 fusion.46
  287.3 0.7 copy-done.47
  287.9 29.0 %all-reduce.21.cloned.1.call-done = bf16[512,1536]{1,0:T(8,128)(2,1)} async-done(((bf16[512,1536]{1,0:T(8,128)(2,1)}), bf16[512,1536]{1,0:T(8,128)(2,1)}) %all-reduce.21.cloned.1.call-update) | async-done | bytes 1572880 | tf_op jit(solution)/shard_map/psum | solution.py:167
  317.0 1.9 convert_element_type.110
  318.9 1.1 fusion.11
  320.5 2.6 gather_fusion.3
  323.1 10.5 %all-to-all-start.2 = ((bf16[64,8,384]{2,1,0:T(8,128)(2,1)}), bf16[64,8,384]{2,1,0:T(8,128)(2,1)S(1)}, u32[]{:S(2)}, u32[]{:S(2)}) async-start(bf16[64,8,384]{2,1,0:T(8,128)(2,1)} %bitcast.7), calls=%async_computation.2 | async-start | bytes 786432 | tf_op jit(solution)/shard_map/all_to_all | solution.py:179
  333.6 0.6 dynamic-slice
  335.1 251.8 %all-reduce.17 = (f32[384]{0:T(512)S(1)}, f32[9,384]{1,0:T(8,128)S(1)}) all-reduce(f32[384]{0:T(512)S(1)} %get-tuple-element.30, f32[9,384]{1,0:T(8,128)S(1)} %stack.39), channel_id=1, replica_groups=mesh['dp'=64,'seq'=4] {'dp'}, use_global_device_ids=true, to_apply=%region_12.13 | all-reduce | flops 3840 | bytes 30720 | tf_op jit(solution)/shard_map/psum | solution.py:175
  586.9 0.6 broadcast_multiply_fusion.4
  587.5 0.6 broadcast_multiply_fusion.3
  588.1 2.6 gather_fusion.4
  590.7 1.6 dynamic-slice_multiply_fusion
  592.3 1.2 copy.21
  593.5 0.8 add_convert_fusion
  594.3 95.7 %reduce-scatter.9.cloned.1.call-done = f32[384,24]{0,1:T(8,128)} async-done(((f32[384,1536]{0,1:T(8,128)}), f32[384,24]{0,1:T(8,128)}) %reduce-scatter.9.cloned.1.call-update) | async-done | bytes 36880
  690.0 1.4 broadcast_multiply_fusion.2
  (173 shorter events, 4.0 us)
Async XLA Ops:
  7.2 22.1 %copy-start.11 = (bf16[512,384]{1,0:T(8,128)(2,1)S(1)}, bf16[512,384]{1,0:T(8,128)(2,1)}, u32[]{:S(2)}) copy-start(bf16[512,384]{1,0:T(8,128)(2,1)} %param.8) | copy-start | bytes 1179652
  10.9 3.2 copy-start.44
  17.1 21.6 %all-to-all-start.1 = ((s32[64,1,8]{2,1,0:T(1,128)}), s32[64,1,8]{2,1,0:T(1,128)S(1)}, u32[]{:S(2)}, u32[]{:S(2)}) async-start(s32[64,1,8]{2,1,0:T(1,128)} %bitcast.4), calls=%async_computation.1 | async-start | bytes 65536 | tf_op jit(solution)/shard_map/all_to_all | solution.py:87
  38.7 19.1 %all-to-all-start = ((bf16[64,8,384]{2,1,0:T(8,128)(2,1)}), bf16[64,8,384]{2,1,0:T(8,128)(2,1)S(1)}, u32[]{:S(2)}, u32[]{:S(2)}) async-start(bf16[64,8,384]{2,1,0:T(8,128)(2,1)} %bitcast.2), calls=%async_computation | async-start | bytes 786432 | tf_op jit(solution)/shard_map/all_to_all | solution.py:86
  43.3 51.4 %all-gather.9.cloned.1.call-start = ((), (), s32[]{:S(2)}) async-start(), calls=%async_computation.8 | async-start | bytes 1966080 | tf_op jit(solution)/shard_map/all_gather | solution.py:90
  44.7 13.1 %copy-start.46 = (s32[512,1]{0,1:T(1,128)}, s32[512,1]{0,1:T(1,128)S(1)}, u32[]{:S(2)}) copy-start(s32[512,1]{0,1:T(1,128)S(1)} %compare_select_fusion) | copy-start | bytes 6148
  57.9 3.4 copy-start.8
  60.5 3.2 copy-start.49
  60.5 3.9 copy-start.48
  60.5 113.0 %all-gather.5.cloned.1.call-start = ((), (), s32[]{:S(2)}) async-start(), calls=%async_computation.5 | async-start | bytes 2396160 | tf_op jit(solution)/shard_map/all_gather | solution.py:98
  61.2 189.3 %all-gather.7.cloned.1.call-start = ((), (), s32[]{:S(2)}) async-start(), calls=%async_computation.6 | async-start | bytes 1198080 | tf_op jit(solution)/shard_map/all_gather | solution.py:99
  61.3 12.8 %collective-permute-start = (bf16[512,384]{1,0:T(8,128)(2,1)S(1)}, bf16[512,384]{1,0:T(8,128)(2,1)S(1)}, u32[]{:S(2)}, u32[]{:S(2)}) collective-permute-start(bf16[512,384]{1,0:T(8,128)(2,1)S(1)} %copy-done.8), channel_id=1, source_target_pairs={{0,1},{1,2},{2,3},{3,0},{4,5},{5,6},{6,7},{7,4},{8,9},{9,10},{10,1... | collective-permute-start | bytes 1179656 | tf_op jit(solution)/shard_map/ppermute | solution.py:124
  62.6 12.9 %collective-permute-start.1 = (bf16[512,384]{1,0:T(8,128)(2,1)S(1)}, bf16[512,384]{1,0:T(8,128)(2,1)S(1)}, u32[]{:S(2)}, u32[]{:S(2)}) collective-permute-start(bf16[512,384]{1,0:T(8,128)(2,1)S(1)} %copy-done.8), channel_id=1, source_target_pairs={{0,3},{1,0},{2,1},{3,2},{4,7},{5,4},{6,5},{7,6},{8,11},{9,8},{10,9... | collective-permute-start | bytes 1179656 | tf_op jit(solution)/shard_map/ppermute | solution.py:129
  63.4 253.5 %all-reduce.21.cloned.1.call-start = ((), (), s32[]{:S(2)}) async-start(), calls=%async_computation.7 | async-start | bytes 3145728 | tf_op jit(solution)/shard_map/psum | solution.py:167
  74.1 19.3 %collective-permute-start.2 = (bf16[512,384]{1,0:T(8,128)(2,1)S(1)}, bf16[512,384]{1,0:T(8,128)(2,1)S(1)}, u32[]{:S(2)}, u32[]{:S(2)}) collective-permute-start(bf16[512,384]{1,0:T(8,128)(2,1)S(1)} %collective-permute-done), channel_id=1, source_target_pairs={{0,1},{1,2},{2,3},{3,0},{4,5},{5,6},{6,7},{7,4},{8,9},{9,10},{10,1... | collective-permute-start | bytes 1179656 | tf_op jit(solution)/shard_map/ppermute | solution.py:124
  93.5 1.2 copy-start.6
  94.7 1.9 copy-start
  96.6 79.1 %copy-start.36 = (f32[512]{0:T(512)}, f32[512]{0:T(512)S(1)}, u32[]{:S(2)}) copy-start(f32[512]{0:T(512)S(1)} %broadcast_multiply_fusion.7) | copy-start | bytes 6148
  173.5 2.2 copy-start.38
  173.5 2.2 copy-start.40
  175.7 2.3 copy-start.4
  178.0 1.3 copy-start.14
  178.0 1.3 copy-start.16
  178.0 1.2 copy-start.18
  178.0 1.2 copy-start.20
  178.0 1.2 copy-start.22
  178.0 1.2 copy-start.24
  178.0 1.2 copy-start.26
  178.0 1.2 copy-start.28
  178.0 1.2 copy-start.30
  178.1 1.2 copy-start.32
  178.1 1.2 copy-start.34
  178.1 1.2 copy-start.42
  178.1 1.2 copy-start.43
  250.6 8.0 %copy-start.15 = (f32[512]{0:T(512)S(1)}, f32[512]{0:T(512)}, u32[]{:S(2)}) copy-start(f32[512]{0:T(512)} %get-tuple-element.47) | copy-start | bytes 6148
  250.6 8.0 %copy-start.17 = (f32[512]{0:T(512)S(1)}, f32[512]{0:T(512)}, u32[]{:S(2)}) copy-start(f32[512]{0:T(512)} %get-tuple-element.48) | copy-start | bytes 6148
  250.6 8.0 %copy-start.19 = (f32[512]{0:T(512)S(1)}, f32[512]{0:T(512)}, u32[]{:S(2)}) copy-start(f32[512]{0:T(512)} %get-tuple-element.49) | copy-start | bytes 6148
  250.6 8.0 %copy-start.21 = (f32[384]{0:T(512)S(1)}, f32[384]{0:T(512)}, u32[]{:S(2)}) copy-start(f32[384]{0:T(512)} %get-tuple-element.17) | copy-start | bytes 4612
  250.6 8.0 %copy-start.23 = (f32[384]{0:T(512)S(1)}, f32[384]{0:T(512)}, u32[]{:S(2)}) copy-start(f32[384]{0:T(512)} %get-tuple-element.18) | copy-start | bytes 4612
  250.6 8.0 %copy-start.25 = (f32[384]{0:T(512)S(1)}, f32[384]{0:T(512)}, u32[]{:S(2)}) copy-start(f32[384]{0:T(512)} %get-tuple-element.19) | copy-start | bytes 4612
  250.6 8.0 %copy-start.27 = (f32[384]{0:T(512)S(1)}, f32[384]{0:T(512)}, u32[]{:S(2)}) copy-start(f32[384]{0:T(512)} %get-tuple-element.20) | copy-start | bytes 4612
  250.6 8.0 %copy-start.29 = (f32[384]{0:T(512)S(1)}, f32[384]{0:T(512)}, u32[]{:S(2)}) copy-start(f32[384]{0:T(512)} %get-tuple-element.21) | copy-start | bytes 4612
  250.6 8.0 %copy-start.31 = (f32[384]{0:T(512)S(1)}, f32[384]{0:T(512)}, u32[]{:S(2)}) copy-start(f32[384]{0:T(512)} %get-tuple-element.22) | copy-start | bytes 4612
  250.6 8.0 %copy-start.33 = (f32[384]{0:T(512)S(1)}, f32[384]{0:T(512)}, u32[]{:S(2)}) copy-start(f32[384]{0:T(512)} %get-tuple-element.23) | copy-start | bytes 4612
  250.6 8.0 %copy-start.35 = (f32[384]{0:T(512)S(1)}, f32[384]{0:T(512)}, u32[]{:S(2)}) copy-start(f32[384]{0:T(512)} %get-tuple-element.25) | copy-start | bytes 4612
  260.2 1.9 copy-start.5
  264.8 325.9 %all-reduce.23.cloned.1.call-start = ((), (), s32[]{:S(2)}) async-start(), calls=%async_computation.10 | async-start | bytes 9437184
  277.9 314.4 %reduce-scatter.7.cloned.1.call-start = ((), (), s32[]{:S(2)}) async-start(), calls=%async_computation.9 | async-start | bytes 1966080
  282.2 1.4 copy-start.7
  282.2 407.8 %reduce-scatter.9.cloned.1.call-start = ((), (), s32[]{:S(2)}) async-start(), calls=%async_computation.11 | async-start | bytes 2396160
  317.0 1.9 copy-start.1
  320.4 13.2 %copy-start.59 = (u32[256]{0:T(256)S(1)}, u32[256]{0:T(256)}, u32[]{:S(2)}) copy-start(u32[256]{0:T(256)} %constant.136) | copy-start | bytes 3076
  320.4 14.4 %copy-start.45 = (s32[512]{0:T(512)S(1)}, s32[512]{0:T(512)}, u32[]{:S(2)}) copy-start(s32[512]{0:T(512)} %copy-done.44) | copy-start | bytes 6148
  320.4 14.4 %copy-start.58 = (f32[384]{0:T(512)S(1)}, f32[384]{0:T(512)}, u32[]{:S(2)}) copy-start(f32[384]{0:T(512)} %get-tuple-element.9) | copy-start | bytes 4612
  320.4 14.4 %copy-start.57 = (f32[384]{0:T(512)S(1)}, f32[384]{0:T(512)}, u32[]{:S(2)}) copy-start(f32[384]{0:T(512)} %get-tuple-element.10) | copy-start | bytes 4612
  320.4 14.4 %copy-start.56 = (f32[384]{0:T(512)S(1)}, f32[384]{0:T(512)}, u32[]{:S(2)}) copy-start(f32[384]{0:T(512)} %get-tuple-element.11) | copy-start | bytes 4612
  320.4 14.5 %copy-start.55 = (f32[384]{0:T(512)S(1)}, f32[384]{0:T(512)}, u32[]{:S(2)}) copy-start(f32[384]{0:T(512)} %get-tuple-element.12) | copy-start | bytes 4612
  320.5 14.5 %copy-start.54 = (f32[384]{0:T(512)S(1)}, f32[384]{0:T(512)}, u32[]{:S(2)}) copy-start(f32[384]{0:T(512)} %get-tuple-element.16) | copy-start | bytes 4612
  320.5 14.5 %copy-start.53 = (f32[384]{0:T(512)S(1)}, f32[384]{0:T(512)}, u32[]{:S(2)}) copy-start(f32[384]{0:T(512)} %get-tuple-element.13) | copy-start | bytes 4612
  320.5 14.5 %copy-start.52 = (f32[384]{0:T(512)S(1)}, f32[384]{0:T(512)}, u32[]{:S(2)}) copy-start(f32[384]{0:T(512)} %get-tuple-element.14) | copy-start | bytes 4612
  320.5 14.5 %copy-start.51 = (f32[384]{0:T(512)S(1)}, f32[384]{0:T(512)}, u32[]{:S(2)}) copy-start(f32[384]{0:T(512)} %get-tuple-element.15) | copy-start | bytes 4612
  320.5 14.5 %copy-start.50 = (f32[384]{0:T(512)S(1)}, f32[384]{0:T(512)}, u32[]{:S(2)}) copy-start(f32[384]{0:T(512)} %get-tuple-element.8) | copy-start | bytes 4612
  323.1 265.0 %all-to-all-start.2 = ((bf16[64,8,384]{2,1,0:T(8,128)(2,1)}), bf16[64,8,384]{2,1,0:T(8,128)(2,1)S(1)}, u32[]{:S(2)}, u32[]{:S(2)}) async-start(bf16[64,8,384]{2,1,0:T(8,128)(2,1)} %bitcast.7), calls=%async_computation.2 | async-start | bytes 786432 | tf_op jit(solution)/shard_map/all_to_all | solution.py:179
  588.1 5.4 copy-start.2
  (9 other events, 8.5 us)
Sparse Core Ops, SparseCore 0:
  60.6 33.2 all-gather.8
  96.6 76.8 all-gather.4
  176.2 74.3 all-gather.6
  264.9 51.9 all-reduce.20
  320.4 201.8 all-reduce.22
  524.7 25.3 reduce-scatter.6
  554.2 135.7 reduce-scatter.8
